TPU v7x, 256 devices: a whole 4x4x8 slice. The times are simulated.
256 devices in a mesh: lat: 16 (over x_hi, y, core), lon: 16 (over z, x_lo).
Axes of the slice: x: 4 (x_hi: 2, x_lo: 2; x = x_hi * 2 + x_lo), y: 4, z: 8, core: 2. Of those that a mesh axis runs over, the one named last changes fastest.
Arguments:
- initial: float32 [64, 256, 2048], P(None, 'lat', 'lon'), may hold values from -6 to 6
- east_wind: float32 [64, 256, 2048], P(None, 'lat', 'lon'), may hold values from -2.5 to 2.5
- north_wind: float32 [64, 256, 2048], P(None, 'lat', 'lon'), may hold values from -2.5 to 2.5
- east_mask: int32 [64, 256, 2048], P(None, 'lat', 'lon'), may hold values from 0 to 1
- north_mask: int32 [64, 256, 2048], P(None, 'lat', 'lon'), may hold values from 0 to 1
- mixing: float32 [63], replicated, may hold values from 0.02 to 0.2
- obs_cell: int32 [16, 16, 4, 256], P('lat', 'lon'), may hold values from 0 to 2047
- obs_level: int32 [16, 16, 4, 256], P('lat', 'lon'), may hold values from 0 to 63
- obs_value: float32 [16, 16, 4, 256], P('lat', 'lon'), may hold values from -6 to 6
- obs_weight: float32 [16, 16, 4, 256], P('lat', 'lon'), may hold values from 0.2 to 2
Outputs:
- gradient: float32 [64, 256, 2048], P(None, 'lat', 'lon')
- cost: float32 [], replicated
Inputs may be any that keep to these rules, and one draw needn't show every extreme that they name: `obs_cell`: row times 128 plus column within the block.
All inputs are finite; a program needn't handle non-finite values.
Results may differ from a plain program's by a relative error of at most 0.0003.
Values sent between devices are 32-bit elements; how exact they have to be, the bound alone decides.
No kernel may reach another device: no remote copies, remote signals or barrier semaphores. Data moves between devices by JAX's collectives and lax.ppermute only.
A program may use at most 64 MiB of HBM per device.

v0:
```python
import jax
import jax.numpy as jnp
from jax import lax
from jax.sharding import PartitionSpec as P

STEPS = 4


def extended(block, sides, width, periodic):
    for axis, dim in sides:
        count = lax.axis_size(axis)
        forward = [(i, i + 1) for i in range(count - 1)]
        if periodic:
            forward.append((count - 1, 0))
        backward = [(target, source) for source, target in forward]
        low = lax.ppermute(
            lax.slice_in_dim(block, block.shape[dim] - width, None, axis=dim), axis, forward
        )
        high = lax.ppermute(lax.slice_in_dim(block, 0, width, axis=dim), axis, backward)
        block = jnp.concatenate([low, block, high], axis=dim)
    return block


def face_parts(velocity, branch):
    share = jnp.where(branch == 1, jnp.where(velocity > 0, 1.0, 0.0), 0.5)
    return (velocity * share, velocity * (1.0 - share))


def vertical(field, mixing):
    flux = mixing[:, None, None] * (field[1:] - field[:-1])
    zero_row = jnp.zeros_like(field[:1])
    return jnp.concatenate([flux, zero_row], 0) - jnp.concatenate([zero_row, flux], 0)


def lon_rim(stacked):
    return extended(stacked, (("lon", 3),), 1, True)


def lat_rim(stacked):
    return extended(stacked, (("lat", 2),), 1, False)


def lat_pair(field):
    widened = lat_rim(field[None])[0]
    return (widened[:, :-2, :], widened[:, 2:, :])


def forward_step(field, west, east, coefs, mixing):
    west_p, west_q, east_p, east_q, south_p, south_q, north_p, north_q = coefs
    south, north = lat_pair(field)
    div_lon = east_p * field + east_q * east - west_p * west - west_q * field
    div_lat = north_p * field + north_q * north - south_p * south - south_q * field
    return field + vertical(field, mixing) - div_lon - div_lat


def reverse_step(adjoint, west, east, coefs, mixing):
    west_p, west_q, east_p, east_q, south_p, south_q, north_p, north_q = coefs
    south, north = lat_pair(adjoint)
    back_lon = -(east_p - west_q) * adjoint - west_q * west + east_p * east
    back_lat = -(north_p - south_q) * adjoint - south_q * south + north_p * north
    return adjoint + vertical(adjoint, mixing) + back_lon + back_lat


def on_device(
    initial,
    east_wind,
    north_wind,
    east_mask,
    north_mask,
    mixing,
    obs_cell,
    obs_level,
    obs_value,
    obs_weight,
):
    levels, rows, cols = initial.shape
    west_p, west_q = face_parts(east_wind, east_mask)
    south_p, south_q = face_parts(north_wind, north_mask)
    global_row = lax.axis_index("lat") * rows + lax.iota(jnp.int32, rows)
    keep = (global_row > 0)[None, :, None]
    south_p = jnp.where(keep, south_p, 0.0)
    south_q = jnp.where(keep, south_q, 0.0)
    flat = obs_level[0, 0] * (rows * cols) + obs_cell[0, 0]
    rim_lon = lon_rim(jnp.stack([west_p, west_q]))
    rim_lat = lat_rim(jnp.stack([south_p, south_q]))
    coefs = (
        west_p,
        west_q,
        rim_lon[0, :, :, 2:],
        rim_lon[1, :, :, 2:],
        south_p,
        south_q,
        rim_lat[0, :, 2:, :],
        rim_lat[1, :, 2:, :],
    )

    def cycle_pair(field):
        widened = lon_rim(field[None])[0]
        return (widened[:, :, :-2], widened[:, :, 2:])

    state = initial
    residues = []
    local_cost = jnp.zeros((), jnp.float32)
    for step in range(STEPS):
        west, east = cycle_pair(state)
        state = forward_step(state, west, east, coefs, mixing)
        innovation = state.reshape(-1)[flat[step]] - obs_value[0, 0, step]
        weighted = obs_weight[0, 0, step] * innovation
        residues.append(weighted)
        local_cost = local_cost + 0.5 * jnp.sum(weighted * innovation)
    adjoint = jnp.zeros_like(initial)
    for step in range(STEPS - 1, -1, -1):
        injected = (
            jnp.zeros((levels * rows * cols,), jnp.float32).at[flat[step]].add(residues[step])
        )
        adjoint = adjoint + injected.reshape(levels, rows, cols)
        west, east = cycle_pair(adjoint)
        adjoint = reverse_step(adjoint, west, east, coefs, mixing)
    cost = lax.psum(local_cost, ("lat", "lon"))
    return (adjoint, cost)


def solution(mesh):
    placed = (
        P(None, "lat", "lon"),
        P(None, "lat", "lon"),
        P(None, "lat", "lon"),
        P(None, "lat", "lon"),
        P(None, "lat", "lon"),
        P(),
        P("lat", "lon", None, None),
        P("lat", "lon", None, None),
        P("lat", "lon", None, None),
        P("lat", "lon", None, None),
    )
    return jax.shard_map(
        on_device,
        mesh=mesh,
        in_specs=placed,
        out_specs=(P(None, "lat", "lon"), P()),
        check_vma=False,
    )
```

profile of v0, /device:TPU:6, one launch (start us, length us, event | category | flops | bytes accessed | tf_op | source)
XLA Modules:
  0.0 336.9 jit_solution(4927736266648225278)
XLA Ops:
  2.9 5.3 %collective-permute-start.3 = (f32[2,64,1,128]{3,2,1,0:T(1,128)S(1)}, f32[2,64,1,128]{3,2,1,0:T(1,128)S(1)}, u32[]{:S(2)}, u32[]{:S(2)}) collective-permute-start(f32[2,64,1,128]{3,2,1,0:T(1,128)S(1)} %pad_maximum_fusion.5), channel_id=1, source_target_pairs={{16,0},{32,16},{48,32},{64,48},{80,64},{96,80},{112,96},{128,112},... | collective-permute-start | bytes 196616 | tf_op jit(solution)/shard_map/ppermute | solution.py:19
  12.3 3.0 collective-permute-start.1
  15.3 4.5 %collective-permute-start.2 = (f32[1,64,16,1]{3,2,1,0:T(8,128)S(1)}, f32[1,64,16,1]{3,2,1,0:T(8,128)S(1)}, u32[]{:S(2)}, u32[]{:S(2)}) collective-permute-start(f32[1,64,16,1]{3,2,1,0:T(8,128)S(1)} %get-tuple-element.50), channel_id=1, source_target_pairs={{1,0},{2,1},{3,2},{4,3},{5,4},{6,5},{7,6},{8,7},{9,8},{10,9},{11,1... | collective-permute-start | bytes 12296 | tf_op jit(solution)/shard_map/ppermute | solution.py:19
  25.5 12.5 %collective-permute-done.1 = f32[1,64,16,1]{3,2,1,0:T(8,128)S(1)} collective-permute-done((f32[1,64,16,1]{3,2,1,0:T(8,128)S(1)}, f32[1,64,16,1]{3,2,1,0:T(8,128)S(1)}, u32[]{:S(2)}, u32[]{:S(2)}) %collective-permute-start.1) | collective-permute-done | bytes 4128 | tf_op jit(solution)/shard_map/ppermute | solution.py:16
  38.1 5.2 %collective-permute-start.5 = (f32[1,64,1,128]{3,2,1,0:T(1,128)S(1)}, f32[1,64,1,128]{3,2,1,0:T(1,128)S(1)}, u32[]{:S(2)}, u32[]{:S(2)}) collective-permute-start(f32[1,64,1,128]{3,2,1,0:T(1,128)S(1)} %get-tuple-element.52), channel_id=1, source_target_pairs={{16,0},{32,16},{48,32},{64,48},{80,64},{96,80},{112,96},{128,112},... | collective-permute-start | bytes 98312 | tf_op jit(solution)/shard_map/ppermute | solution.py:19
  47.5 4.4 %fusion.53 = (f32[64,16,128]{2,1,0:T(8,128)S(1)}, f32[64,16,128]{2,1,0:T(8,128)S(1)}, f32[64,16,128]{2,1,0:T(8,128)}, f32[64,16,128]{2,1,0:T(8,128)}, f32[64,16,128]{2,1,0:T(8,128)S(1)}) fusion(f32[64,18,128]{2,1,0:T(8,128)S(1)} %maximum_bitcast_fusion.8, f32[64,16,130]{2,1,0:T(8,128)} %maximum_bitcast_fusion, f32[64,16,128]{2,1,0:T(8,128)S(1)} %multiply_select_fusion, ...), kind=kLoop, calls=%fused_computation.107 | loop fusion | flops 4849664 | bytes 9764880 | tf_op jit(solution)/shard_map/sub | solution.py:53
  57.9 7.3 %collective-permute-start.9 = (f32[1,64,1,128]{3,2,1,0:T(1,128)S(1)}, f32[1,64,1,128]{3,2,1,0:T(1,128)S(1)}, u32[]{:S(2)}, u32[]{:S(2)}) collective-permute-start(f32[1,64,1,128]{3,2,1,0:T(1,128)S(1)} %get-tuple-element.48), channel_id=1, source_target_pairs={{16,0},{32,16},{48,32},{64,48},{80,64},{96,80},{112,96},{128,112},... | collective-permute-start | bytes 98312 | tf_op jit(solution)/shard_map/ppermute | solution.py:19
  67.7 8.7 %collective-permute-done.6 = f32[1,64,16,1]{3,2,1,0:T(8,128)S(1)} collective-permute-done((f32[1,64,16,1]{3,2,1,0:T(8,128)}, f32[1,64,16,1]{3,2,1,0:T(8,128)S(1)}, u32[]{:S(2)}, u32[]{:S(2)}) %collective-permute-start.6) | collective-permute-done | bytes 4128 | tf_op jit(solution)/shard_map/ppermute | solution.py:16
  78.0 3.3 collective-permute-done.8
  88.1 7.4 %collective-permute-start.13 = (f32[1,64,1,128]{3,2,1,0:T(1,128)S(1)}, f32[1,64,1,128]{3,2,1,0:T(1,128)S(1)}, u32[]{:S(2)}, u32[]{:S(2)}) collective-permute-start(f32[1,64,1,128]{3,2,1,0:T(1,128)S(1)} %get-tuple-element.44), channel_id=1, source_target_pairs={{16,0},{32,16},{48,32},{64,48},{80,64},{96,80},{112,96},{128,112},... | collective-permute-start | bytes 98312 | tf_op jit(solution)/shard_map/ppermute | solution.py:19
  100.7 2.9 scatter_custom_fusion.2
  118.9 7.3 %collective-permute-start.17 = (f32[1,64,1,128]{3,2,1,0:T(1,128)S(1)}, f32[1,64,1,128]{3,2,1,0:T(1,128)S(1)}, u32[]{:S(2)}, u32[]{:S(2)}) collective-permute-start(f32[1,64,1,128]{3,2,1,0:T(1,128)S(1)} %get-tuple-element.40), channel_id=1, source_target_pairs={{16,0},{32,16},{48,32},{64,48},{80,64},{96,80},{112,96},{128,112},... | collective-permute-start | bytes 98312 | tf_op jit(solution)/shard_map/ppermute | solution.py:19
  138.0 4.5 %collective-permute-done.16 = f32[1,64,1,128]{3,2,1,0:T(1,128)S(1)} collective-permute-done((f32[1,64,1,128]{3,2,1,0:T(1,128)S(1)}, f32[1,64,1,128]{3,2,1,0:T(1,128)S(1)}, u32[]{:S(2)}, u32[]{:S(2)}) %collective-permute-start.16) | collective-permute-done | bytes 32800 | tf_op jit(solution)/shard_map/ppermute | solution.py:16
  152.6 88.8 %psum.7 = f32[]{:T(128)} all-reduce(f32[]{:T(128)S(6)} %add.261), channel_id=1, replica_groups=mesh['lat'=16,'lon'=16] {'lat','lon'}, use_global_device_ids=true, to_apply=%region_8.9 | all-reduce | flops 1 | bytes 8 | tf_op jit(solution)/shard_map/psum | solution.py:119
  243.4 7.2 %collective-permute-start.21 = (f32[1,64,1,128]{3,2,1,0:T(1,128)S(1)}, f32[1,64,1,128]{3,2,1,0:T(1,128)S(1)}, u32[]{:S(2)}, u32[]{:S(2)}) collective-permute-start(f32[1,64,1,128]{3,2,1,0:T(1,128)S(1)} %get-tuple-element.36), channel_id=1, source_target_pairs={{16,0},{32,16},{48,32},{64,48},{80,64},{96,80},{112,96},{128,112},... | collective-permute-start | bytes 98312 | tf_op jit(solution)/shard_map/ppermute | solution.py:19
  258.9 7.3 %collective-permute-start.25 = (f32[1,64,1,128]{3,2,1,0:T(1,128)S(1)}, f32[1,64,1,128]{3,2,1,0:T(1,128)S(1)}, u32[]{:S(2)}, u32[]{:S(2)}) collective-permute-start(f32[1,64,1,128]{3,2,1,0:T(1,128)S(1)} %get-tuple-element.32), channel_id=1, source_target_pairs={{16,0},{32,16},{48,32},{64,48},{80,64},{96,80},{112,96},{128,112},... | collective-permute-start | bytes 98312 | tf_op jit(solution)/shard_map/ppermute | solution.py:19
  266.1 10.9 %collective-permute-done.22 = f32[1,64,16,1]{3,2,1,0:T(8,128)S(1)} collective-permute-done((f32[1,64,16,1]{3,2,1,0:T(8,128)S(1)}, f32[1,64,16,1]{3,2,1,0:T(8,128)S(1)}, u32[]{:S(2)}, u32[]{:S(2)}) %collective-permute-start.22) | collective-permute-done | bytes 4128 | tf_op jit(solution)/shard_map/ppermute | solution.py:16
  277.5 3.9 %collective-permute-done.24 = f32[1,64,1,128]{3,2,1,0:T(1,128)S(1)} collective-permute-done((f32[1,64,1,128]{3,2,1,0:T(1,128)S(1)}, f32[1,64,1,128]{3,2,1,0:T(1,128)S(1)}, u32[]{:S(2)}, u32[]{:S(2)}) %collective-permute-start.24) | collective-permute-done | bytes 32800 | tf_op jit(solution)/shard_map/ppermute | solution.py:16
  286.5 7.3 %collective-permute-start.29 = (f32[1,64,1,128]{3,2,1,0:T(1,128)S(1)}, f32[1,64,1,128]{3,2,1,0:T(1,128)S(1)}, u32[]{:S(2)}, u32[]{:S(2)}) collective-permute-start(f32[1,64,1,128]{3,2,1,0:T(1,128)S(1)} %get-tuple-element.28), channel_id=1, source_target_pairs={{16,0},{32,16},{48,32},{64,48},{80,64},{96,80},{112,96},{128,112},... | collective-permute-start | bytes 98312 | tf_op jit(solution)/shard_map/ppermute | solution.py:19
  293.8 10.8 %collective-permute-done.26 = f32[1,64,16,1]{3,2,1,0:T(8,128)S(1)} collective-permute-done((f32[1,64,16,1]{3,2,1,0:T(8,128)S(1)}, f32[1,64,16,1]{3,2,1,0:T(8,128)S(1)}, u32[]{:S(2)}, u32[]{:S(2)}) %collective-permute-start.26) | collective-permute-done | bytes 4128 | tf_op jit(solution)/shard_map/ppermute | solution.py:16
  305.1 3.4 collective-permute-done.28
  313.6 7.3 %collective-permute-start.33 = (f32[1,64,1,128]{3,2,1,0:T(1,128)S(1)}, f32[1,64,1,128]{3,2,1,0:T(1,128)S(1)}, u32[]{:S(2)}, u32[]{:S(2)}) collective-permute-start(f32[1,64,1,128]{3,2,1,0:T(1,128)S(1)} %get-tuple-element.24), channel_id=1, source_target_pairs={{16,0},{32,16},{48,32},{64,48},{80,64},{96,80},{112,96},{128,112},... | collective-permute-start | bytes 98312 | tf_op jit(solution)/shard_map/ppermute | solution.py:19
  320.8 9.5 %collective-permute-done.30 = f32[1,64,16,1]{3,2,1,0:T(8,128)S(1)} collective-permute-done((f32[1,64,16,1]{3,2,1,0:T(8,128)S(1)}, f32[1,64,16,1]{3,2,1,0:T(8,128)S(1)}, u32[]{:S(2)}, u32[]{:S(2)}) %collective-permute-start.30) | collective-permute-done | bytes 4128 | tf_op jit(solution)/shard_map/ppermute | solution.py:16
  330.8 4.6 %collective-permute-done.32 = f32[1,64,1,128]{3,2,1,0:T(1,128)S(1)} collective-permute-done((f32[1,64,1,128]{3,2,1,0:T(1,128)S(1)}, f32[1,64,1,128]{3,2,1,0:T(1,128)S(1)}, u32[]{:S(2)}, u32[]{:S(2)}) %collective-permute-start.32) | collective-permute-done | bytes 32800 | tf_op jit(solution)/shard_map/ppermute | solution.py:16
  (200 shorter events, 95.6 us)
Async XLA Ops:
  2.9 43.5 %collective-permute-start.3 = (f32[2,64,1,128]{3,2,1,0:T(1,128)S(1)}, f32[2,64,1,128]{3,2,1,0:T(1,128)S(1)}, u32[]{:S(2)}, u32[]{:S(2)}) collective-permute-start(f32[2,64,1,128]{3,2,1,0:T(1,128)S(1)} %pad_maximum_fusion.5), channel_id=1, source_target_pairs={{16,0},{32,16},{48,32},{64,48},{80,64},{96,80},{112,96},{128,112},... | collective-permute-start | bytes 196616 | tf_op jit(solution)/shard_map/ppermute | solution.py:19
  12.0 32.8 %collective-permute-start = (f32[2,64,16,1]{1,2,3,0:T(8,128)S(1)}, f32[2,64,16,1]{1,2,3,0:T(8,128)S(1)}, u32[]{:S(2)}, u32[]{:S(2)}) collective-permute-start(f32[2,64,16,1]{1,2,3,0:T(8,128)S(1)} %copy.29), channel_id=1, source_target_pairs={{1,0},{2,1},{3,2},{4,3},{5,4},{6,5},{7,6},{8,7},{9,8},{10,9},{11,1... | collective-permute-start | bytes 24584 | tf_op jit(solution)/shard_map/ppermute | solution.py:19
  12.3 25.8 %collective-permute-start.1 = (f32[1,64,16,1]{3,2,1,0:T(8,128)S(1)}, f32[1,64,16,1]{3,2,1,0:T(8,128)S(1)}, u32[]{:S(2)}, u32[]{:S(2)}) collective-permute-start(f32[1,64,16,1]{3,2,1,0:T(8,128)S(1)} %get-tuple-element.49), channel_id=1, source_target_pairs={{0,1},{1,2},{2,3},{3,4},{4,5},{5,6},{6,7},{7,8},{8,9},{9,10},{10,1... | collective-permute-start | bytes 12296 | tf_op jit(solution)/shard_map/ppermute | solution.py:16
  15.3 28.0 %collective-permute-start.2 = (f32[1,64,16,1]{3,2,1,0:T(8,128)S(1)}, f32[1,64,16,1]{3,2,1,0:T(8,128)S(1)}, u32[]{:S(2)}, u32[]{:S(2)}) collective-permute-start(f32[1,64,16,1]{3,2,1,0:T(8,128)S(1)} %get-tuple-element.50), channel_id=1, source_target_pairs={{1,0},{2,1},{3,2},{4,3},{5,4},{6,5},{7,6},{8,7},{9,8},{10,9},{11,1... | collective-permute-start | bytes 12296 | tf_op jit(solution)/shard_map/ppermute | solution.py:19
  19.8 26.4 %collective-permute-start.4 = (f32[1,64,1,128]{3,2,1,0:T(1,128)S(1)}, f32[1,64,1,128]{3,2,1,0:T(1,128)S(1)}, u32[]{:S(2)}, u32[]{:S(2)}) collective-permute-start(f32[1,64,1,128]{3,2,1,0:T(1,128)S(1)} %get-tuple-element.51), channel_id=1, source_target_pairs={{0,16},{16,32},{32,48},{48,64},{64,80},{80,96},{96,112},{112,128},... | collective-permute-start | bytes 98312 | tf_op jit(solution)/shard_map/ppermute | solution.py:16
  53.9 22.4 %collective-permute-start.6 = (f32[1,64,16,1]{3,2,1,0:T(8,128)}, f32[1,64,16,1]{3,2,1,0:T(8,128)S(1)}, u32[]{:S(2)}, u32[]{:S(2)}) collective-permute-start(f32[1,64,16,1]{3,2,1,0:T(8,128)} %get-tuple-element.45), channel_id=1, source_target_pairs={{0,1},{1,2},{2,3},{3,4},{4,5},{5,6},{6,7},{7,8},{8,9},{9,10},{10,1... | collective-permute-start | bytes 12296 | tf_op jit(solution)/shard_map/ppermute | solution.py:16
  53.9 22.4 %collective-permute-start.7 = (f32[1,64,16,1]{3,2,1,0:T(8,128)}, f32[1,64,16,1]{3,2,1,0:T(8,128)}, u32[]{:S(2)}, u32[]{:S(2)}) collective-permute-start(f32[1,64,16,1]{3,2,1,0:T(8,128)} %get-tuple-element.46), channel_id=1, source_target_pairs={{1,0},{2,1},{3,2},{4,3},{5,4},{6,5},{7,6},{8,7},{9,8},{10,9},{11,1... | collective-permute-start | bytes 12296 | tf_op jit(solution)/shard_map/ppermute | solution.py:19
  56.0 25.3 %collective-permute-start.8 = (f32[1,64,1,128]{3,2,1,0:T(1,128)S(1)}, f32[1,64,1,128]{3,2,1,0:T(1,128)S(1)}, u32[]{:S(2)}, u32[]{:S(2)}) collective-permute-start(f32[1,64,1,128]{3,2,1,0:T(1,128)S(1)} %get-tuple-element.47), channel_id=1, source_target_pairs={{0,16},{16,32},{32,48},{48,64},{64,80},{80,96},{96,112},{112,128},... | collective-permute-start | bytes 98312 | tf_op jit(solution)/shard_map/ppermute | solution.py:16
  57.9 23.4 %collective-permute-start.9 = (f32[1,64,1,128]{3,2,1,0:T(1,128)S(1)}, f32[1,64,1,128]{3,2,1,0:T(1,128)S(1)}, u32[]{:S(2)}, u32[]{:S(2)}) collective-permute-start(f32[1,64,1,128]{3,2,1,0:T(1,128)S(1)} %get-tuple-element.48), channel_id=1, source_target_pairs={{16,0},{32,16},{48,32},{64,48},{80,64},{96,80},{112,96},{128,112},... | collective-permute-start | bytes 98312 | tf_op jit(solution)/shard_map/ppermute | solution.py:19
  84.2 23.6 %collective-permute-start.10 = (f32[1,64,16,1]{3,2,1,0:T(8,128)}, f32[1,64,16,1]{3,2,1,0:T(8,128)S(1)}, u32[]{:S(2)}, u32[]{:S(2)}) collective-permute-start(f32[1,64,16,1]{3,2,1,0:T(8,128)} %get-tuple-element.41), channel_id=1, source_target_pairs={{0,1},{1,2},{2,3},{3,4},{4,5},{5,6},{6,7},{7,8},{8,9},{9,10},{10,1... | collective-permute-start | bytes 12296 | tf_op jit(solution)/shard_map/ppermute | solution.py:16
  84.2 23.6 %collective-permute-start.11 = (f32[1,64,16,1]{3,2,1,0:T(8,128)}, f32[1,64,16,1]{3,2,1,0:T(8,128)}, u32[]{:S(2)}, u32[]{:S(2)}) collective-permute-start(f32[1,64,16,1]{3,2,1,0:T(8,128)} %get-tuple-element.42), channel_id=1, source_target_pairs={{1,0},{2,1},{3,2},{4,3},{5,4},{6,5},{7,6},{8,7},{9,8},{10,9},{11,1... | collective-permute-start | bytes 12296 | tf_op jit(solution)/shard_map/ppermute | solution.py:19
  86.2 25.8 %collective-permute-start.12 = (f32[1,64,1,128]{3,2,1,0:T(1,128)S(1)}, f32[1,64,1,128]{3,2,1,0:T(1,128)S(1)}, u32[]{:S(2)}, u32[]{:S(2)}) collective-permute-start(f32[1,64,1,128]{3,2,1,0:T(1,128)S(1)} %get-tuple-element.43), channel_id=1, source_target_pairs={{0,16},{16,32},{32,48},{48,64},{64,80},{80,96},{96,112},{112,128},... | collective-permute-start | bytes 98312 | tf_op jit(solution)/shard_map/ppermute | solution.py:16
  88.1 23.9 %collective-permute-start.13 = (f32[1,64,1,128]{3,2,1,0:T(1,128)S(1)}, f32[1,64,1,128]{3,2,1,0:T(1,128)S(1)}, u32[]{:S(2)}, u32[]{:S(2)}) collective-permute-start(f32[1,64,1,128]{3,2,1,0:T(1,128)S(1)} %get-tuple-element.44), channel_id=1, source_target_pairs={{16,0},{32,16},{48,32},{64,48},{80,64},{96,80},{112,96},{128,112},... | collective-permute-start | bytes 98312 | tf_op jit(solution)/shard_map/ppermute | solution.py:19
  117.0 25.5 %collective-permute-start.16 = (f32[1,64,1,128]{3,2,1,0:T(1,128)S(1)}, f32[1,64,1,128]{3,2,1,0:T(1,128)S(1)}, u32[]{:S(2)}, u32[]{:S(2)}) collective-permute-start(f32[1,64,1,128]{3,2,1,0:T(1,128)S(1)} %get-tuple-element.39), channel_id=1, source_target_pairs={{0,16},{16,32},{32,48},{48,64},{64,80},{80,96},{96,112},{112,128},... | collective-permute-start | bytes 98312 | tf_op jit(solution)/shard_map/ppermute | solution.py:16
  118.9 23.6 %collective-permute-start.17 = (f32[1,64,1,128]{3,2,1,0:T(1,128)S(1)}, f32[1,64,1,128]{3,2,1,0:T(1,128)S(1)}, u32[]{:S(2)}, u32[]{:S(2)}) collective-permute-start(f32[1,64,1,128]{3,2,1,0:T(1,128)S(1)} %get-tuple-element.40), channel_id=1, source_target_pairs={{16,0},{32,16},{48,32},{64,48},{80,64},{96,80},{112,96},{128,112},... | collective-permute-start | bytes 98312 | tf_op jit(solution)/shard_map/ppermute | solution.py:19
  149.7 100.9 %collective-permute-start.18 = (f32[1,64,16,1]{3,2,1,0:T(8,128)}, f32[1,64,16,1]{3,2,1,0:T(8,128)}, u32[]{:S(2)}, u32[]{:S(2)}) collective-permute-start(f32[1,64,16,1]{3,2,1,0:T(8,128)} %get-tuple-element.33), channel_id=1, source_target_pairs={{0,1},{1,2},{2,3},{3,4},{4,5},{5,6},{6,7},{7,8},{8,9},{9,10},{10,1... | collective-permute-start | bytes 12296 | tf_op jit(solution)/shard_map/ppermute | solution.py:16
  149.7 100.9 %collective-permute-start.19 = (f32[1,64,16,1]{3,2,1,0:T(8,128)}, f32[1,64,16,1]{3,2,1,0:T(8,128)}, u32[]{:S(2)}, u32[]{:S(2)}) collective-permute-start(f32[1,64,16,1]{3,2,1,0:T(8,128)} %get-tuple-element.34), channel_id=1, source_target_pairs={{1,0},{2,1},{3,2},{4,3},{5,4},{6,5},{7,6},{8,7},{9,8},{10,9},{11,1... | collective-permute-start | bytes 12296 | tf_op jit(solution)/shard_map/ppermute | solution.py:19
  254.3 22.7 %collective-permute-start.22 = (f32[1,64,16,1]{3,2,1,0:T(8,128)S(1)}, f32[1,64,16,1]{3,2,1,0:T(8,128)S(1)}, u32[]{:S(2)}, u32[]{:S(2)}) collective-permute-start(f32[1,64,16,1]{3,2,1,0:T(8,128)S(1)} %get-tuple-element.29), channel_id=1, source_target_pairs={{0,1},{1,2},{2,3},{3,4},{4,5},{5,6},{6,7},{7,8},{8,9},{9,10},{10,1... | collective-permute-start | bytes 12296 | tf_op jit(solution)/shard_map/ppermute | solution.py:16
  256.9 24.5 %collective-permute-start.24 = (f32[1,64,1,128]{3,2,1,0:T(1,128)S(1)}, f32[1,64,1,128]{3,2,1,0:T(1,128)S(1)}, u32[]{:S(2)}, u32[]{:S(2)}) collective-permute-start(f32[1,64,1,128]{3,2,1,0:T(1,128)S(1)} %get-tuple-element.31), channel_id=1, source_target_pairs={{0,16},{16,32},{32,48},{48,64},{64,80},{80,96},{96,112},{112,128},... | collective-permute-start | bytes 98312 | tf_op jit(solution)/shard_map/ppermute | solution.py:16
  258.9 22.5 %collective-permute-start.25 = (f32[1,64,1,128]{3,2,1,0:T(1,128)S(1)}, f32[1,64,1,128]{3,2,1,0:T(1,128)S(1)}, u32[]{:S(2)}, u32[]{:S(2)}) collective-permute-start(f32[1,64,1,128]{3,2,1,0:T(1,128)S(1)} %get-tuple-element.32), channel_id=1, source_target_pairs={{16,0},{32,16},{48,32},{64,48},{80,64},{96,80},{112,96},{128,112},... | collective-permute-start | bytes 98312 | tf_op jit(solution)/shard_map/ppermute | solution.py:19
  282.4 22.1 %collective-permute-start.26 = (f32[1,64,16,1]{3,2,1,0:T(8,128)S(1)}, f32[1,64,16,1]{3,2,1,0:T(8,128)S(1)}, u32[]{:S(2)}, u32[]{:S(2)}) collective-permute-start(f32[1,64,16,1]{3,2,1,0:T(8,128)S(1)} %get-tuple-element.25), channel_id=1, source_target_pairs={{0,1},{1,2},{2,3},{3,4},{4,5},{5,6},{6,7},{7,8},{8,9},{9,10},{10,1... | collective-permute-start | bytes 12296 | tf_op jit(solution)/shard_map/ppermute | solution.py:16
  282.5 22.0 %collective-permute-start.27 = (f32[1,64,16,1]{3,2,1,0:T(8,128)S(1)}, f32[1,64,16,1]{3,2,1,0:T(8,128)S(1)}, u32[]{:S(2)}, u32[]{:S(2)}) collective-permute-start(f32[1,64,16,1]{3,2,1,0:T(8,128)S(1)} %get-tuple-element.26), channel_id=1, source_target_pairs={{1,0},{2,1},{3,2},{4,3},{5,4},{6,5},{7,6},{8,7},{9,8},{10,9},{11,1... | collective-permute-start | bytes 12296 | tf_op jit(solution)/shard_map/ppermute | solution.py:19
  284.6 23.8 %collective-permute-start.28 = (f32[1,64,1,128]{3,2,1,0:T(1,128)S(1)}, f32[1,64,1,128]{3,2,1,0:T(1,128)S(1)}, u32[]{:S(2)}, u32[]{:S(2)}) collective-permute-start(f32[1,64,1,128]{3,2,1,0:T(1,128)S(1)} %get-tuple-element.27), channel_id=1, source_target_pairs={{0,16},{16,32},{32,48},{48,64},{64,80},{80,96},{96,112},{112,128},... | collective-permute-start | bytes 98312 | tf_op jit(solution)/shard_map/ppermute | solution.py:16
  311.6 23.7 %collective-permute-start.32 = (f32[1,64,1,128]{3,2,1,0:T(1,128)S(1)}, f32[1,64,1,128]{3,2,1,0:T(1,128)S(1)}, u32[]{:S(2)}, u32[]{:S(2)}) collective-permute-start(f32[1,64,1,128]{3,2,1,0:T(1,128)S(1)} %get-tuple-element.23), channel_id=1, source_target_pairs={{0,16},{16,32},{32,48},{48,64},{64,80},{80,96},{96,112},{112,128},... | collective-permute-start | bytes 98312 | tf_op jit(solution)/shard_map/ppermute | solution.py:16
  (49 other events, 277.9 us)
where the time goes:
time: 338 us; the launch traced here: 337 us
  starting transfers between devices  99.4 us (29%)
  blocking collectives  88.8 us (26%)
  waiting for transfers between devices  77.1 us (23%)
  other arithmetic  42.9 us (13%)
  local copies, waits for them, and re-layouts  24.5 us (7%)
  between operations  4.14 us (1%)
    psum x1, blocking collectives, on_device(): cost = lax.psum(local_cost, ('lat', 'lon'))  88.8 us
    ppermute x18, starting transfers between devices, extended(): lax.ppermute(lax.slice_in_dim(block, 0, width, axis=dim), axis, backward)  78 us
    ppermute x16, waiting for transfers between devices, extended(): lax.ppermute(lax.slice_in_dim(block, block.shape[dim] - width, None, axis...  76.3 us
    ppermute x16, starting transfers between devices, extended(): lax.ppermute(lax.slice_in_dim(block, block.shape[dim] - width, None, axis...  21.4 us
    scatter-add x4, other arithmetic, on_device(): jnp.zeros((levels * rows * cols,), jnp.float32).at[flat[step]]  10.8 us
    squeeze x8, other arithmetic, cycle_pair(): widened = lon_rim(field[None])[0]  9.39 us
    gather x4, local copies, waits for them, and re-layouts, on_device(): innovation = state.reshape(-1)[flat[step]] - obs_value[0, 0, step]  8.98 us
  transfers between devices with their start and end apart: 34, of which 13 were waited for; matrix products, arithmetic and copies ran while one was open for 11% of the time, Pallas kernels for 0%

commit v1 on v0

v1 whole, which is shorter than its diff:
```python
import jax
import jax.numpy as jnp
from jax import lax
from jax.sharding import PartitionSpec as P

STEPS = 4
HALO = 2 * STEPS


def face_parts(velocity, branch):
    share = jnp.where(branch == 1, jnp.where(velocity > 0, 1.0, 0.0), 0.5)
    return (velocity * share, velocity * (1.0 - share))


def vertical(field, mixing):
    flux = mixing[:, None, None] * (field[1:] - field[:-1])
    zero_row = jnp.zeros_like(field[:1])
    return jnp.concatenate([flux, zero_row], 0) - jnp.concatenate([zero_row, flux], 0)


def swap(block, axis, width, dim, periodic, extra):
    count = lax.axis_size(axis)
    forward = [(i, i + 1) for i in range(count - 1)]
    if periodic:
        forward.append((count - 1, 0))
    backward = [(t, s) for s, t in forward]
    size = block.shape[dim]
    hi = lax.slice_in_dim(block, size - width, size, axis=dim)
    lo = lax.slice_in_dim(block, 0, width, axis=dim)
    n = hi.size
    low = lax.ppermute(jnp.concatenate([hi.reshape(-1), extra]), axis, forward)
    high = lax.ppermute(jnp.concatenate([lo.reshape(-1), extra]), axis, backward)
    shape = hi.shape
    grown = jnp.concatenate([low[:n].reshape(shape), block, high[:n].reshape(shape)], axis=dim)
    return grown, low[n:], high[n:]


def on_device(
    initial,
    east_wind,
    north_wind,
    east_mask,
    north_mask,
    mixing,
    obs_cell,
    obs_level,
    obs_value,
    obs_weight,
):
    levels, rows, cols = initial.shape
    h = HALO
    west_p, west_q = face_parts(east_wind, east_mask)
    south_p, south_q = face_parts(north_wind, north_mask)
    global_row = lax.axis_index("lat") * rows + lax.iota(jnp.int32, rows)
    keep = (global_row > 0)[None, :, None]
    south_p = jnp.where(keep, south_p, 0.0)
    south_q = jnp.where(keep, south_q, 0.0)

    fields = jnp.stack([initial, west_p, west_q, south_p, south_q])
    obs = jnp.stack(
        [
            obs_cell[0, 0].astype(jnp.float32),
            obs_level[0, 0].astype(jnp.float32),
            obs_value[0, 0],
            obs_weight[0, 0],
        ]
    ).reshape(-1)
    fields, obs_w, obs_e = swap(fields, "lon", h, 3, True, obs)
    row_obs = jnp.concatenate([obs_w, obs, obs_e])
    fields, obs_s, obs_n = swap(fields, "lat", h, 2, False, row_obs)

    state = fields[0]
    west_p, west_q, south_p, south_q = fields[1], fields[2], fields[3], fields[4]
    east_p = jnp.roll(west_p, -1, 2)
    east_q = jnp.roll(west_q, -1, 2)
    north_p = jnp.roll(south_p, -1, 1)
    north_q = jnp.roll(south_q, -1, 1)
    ext_rows, ext_cols = rows + 2 * h, cols + 2 * h

    sets = []
    for dr, payload in ((-1, obs_s), (0, row_obs), (1, obs_n)):
        parts = payload.reshape(3, 4, STEPS, -1)
        for j, dc in enumerate((-1, 0, 1)):
            sets.append((dr, dc, parts[j]))
    cells = jnp.stack([p[0] for _, _, p in sets]).astype(jnp.int32)
    lev = jnp.stack([p[1] for _, _, p in sets]).astype(jnp.int32)
    val = jnp.stack([p[2] for _, _, p in sets])
    wgt = jnp.stack([p[3] for _, _, p in sets])
    dr = jnp.array([s[0] for s in sets], jnp.int32)[:, None, None]
    dc = jnp.array([s[1] for s in sets], jnp.int32)[:, None, None]
    own = jnp.array([s[0] == 0 and s[1] == 0 for s in sets])[:, None, None]
    er = dr * rows + cells // cols + h
    ec = dc * cols + cells % cols + h

    def forward_step(field):
        west = jnp.roll(field, 1, 2)
        east = jnp.roll(field, -1, 2)
        south = jnp.roll(field, 1, 1)
        north = jnp.roll(field, -1, 1)
        div_lon = east_p * field + east_q * east - west_p * west - west_q * field
        div_lat = north_p * field + north_q * north - south_p * south - south_q * field
        return field + vertical(field, mixing) - div_lon - div_lat

    def reverse_step(adjoint):
        west = jnp.roll(adjoint, 1, 2)
        east = jnp.roll(adjoint, -1, 2)
        south = jnp.roll(adjoint, 1, 1)
        north = jnp.roll(adjoint, -1, 1)
        back_lon = -(east_p - west_q) * adjoint - west_q * west + east_p * east
        back_lat = -(north_p - south_q) * adjoint - south_q * south + north_p * north
        return adjoint + vertical(adjoint, mixing) + back_lon + back_lat

    local_cost = jnp.zeros((), jnp.float32)
    injections = []
    for step in range(STEPS):
        state = forward_step(state)
        k = step + 1
        valid = (er[:, step] >= k) & (er[:, step] < ext_rows - k)
        valid = valid & (ec[:, step] >= k) & (ec[:, step] < ext_cols - k)
        li = jnp.where(valid, lev[:, step], 0)
        ri = jnp.where(valid, er[:, step], 0)
        ci = jnp.where(valid, ec[:, step], 0)
        picked = state[li, ri, ci]
        innovation = picked - val[:, step]
        weighted = jnp.where(valid, wgt[:, step] * innovation, 0.0)
        mine = own[:, 0]
        local_cost = local_cost + 0.5 * jnp.sum(jnp.where(mine, weighted * innovation, 0.0))
        injections.append(
            jnp.zeros((levels, ext_rows, ext_cols), jnp.float32).at[li, ri, ci].add(weighted)
        )
    adjoint = jnp.zeros((levels, ext_rows, ext_cols), jnp.float32)
    for step in range(STEPS - 1, -1, -1):
        adjoint = reverse_step(adjoint + injections[step])
    gradient = adjoint[:, h : h + rows, h : h + cols]
    cost = lax.psum(local_cost, ("lat", "lon"))
    return (gradient, cost)


def solution(mesh):
    placed = (
        P(None, "lat", "lon"),
        P(None, "lat", "lon"),
        P(None, "lat", "lon"),
        P(None, "lat", "lon"),
        P(None, "lat", "lon"),
        P(),
        P("lat", "lon", None, None),
        P("lat", "lon", None, None),
        P("lat", "lon", None, None),
        P("lat", "lon", None, None),
    )
    return jax.shard_map(
        on_device,
        mesh=mesh,
        in_specs=placed,
        out_specs=(P(None, "lat", "lon"), P()),
        check_vma=False,
    )
```

time: 338 us -> 679 us (2.01); the launches traced: 337 us -> 668 us
  local copies, waits for them, and re-layouts: 24.5 us -> 366 us
  other arithmetic: 42.9 us -> 184 us
  starting transfers between devices: 99.4 us -> 12.5 us
  waiting for transfers between devices: 77.1 us -> 20.3 us
  blocking collectives: 88.8 us -> 80 us
    gather x4 -> x8, local copies, waits for them, and re-layouts: 8.98 us -> 204 us  [on_device(): picked = state[li, ri, ci]]
    ppermute x34 -> x4, starting transfers between devices: 99.4 us -> 12.5 us  [the longest x2 8.37 us: swap(): lax.ppermute(jnp.concatenate([lo.reshape(-1), extra]), axis, backward)]
    slice x19 -> x61, local copies, waits for them, and re-layouts: 8.61 us -> 89 us  [the longest x6 17.2 us: reverse_step(): east = jnp.roll(adjoint, -1, 2)]
    unnamed x0 -> x13, other arithmetic: none -> 66.9 us
    ppermute x34 -> x4, waiting for transfers between devices: 77.1 us -> 20.3 us  [the longest x2 16.1 us: swap(): low = lax.ppermute(jnp.concatenate([hi.reshape(-1), extra]), axis, forward)]
    sub x4, other arithmetic: 6.35 us -> 43 us  [forward_step(): return field + vertical(field, mixing) - div_lon - div_lat]
    reshape x0 -> x8, local copies, waits for them, and re-layouts: none -> 27.3 us  [the longest x2 6.91 us: swap(): low[:n].reshape(shape)]
    add x1 -> x3, other arithmetic: 1.35 us -> 22.9 us  [reverse_step(): return adjoint + vertical(adjoint, mixing) + back_lon + back_lat]
  transfers between devices with their start and end apart: 34 -> 4, of which waited for: 13 -> 3; matrix products, arithmetic and copies ran while one was open for 11% -> 2% of each run, Pallas kernels for 0% -> 0%
where the time goes in v1:
time: 679 us; the launch traced here: 668 us
  local copies, waits for them, and re-layouts  366 us (54%)
  other arithmetic  184 us (27%)
  blocking collectives  80 us (12%)
  waiting for transfers between devices  20.3 us (3%)
  starting transfers between devices  12.5 us (2%)
    gather x8, local copies, waits for them, and re-layouts, on_device(): picked = state[li, ri, ci]  204 us
    psum x1, blocking collectives, on_device(): cost = lax.psum(local_cost, ('lat', 'lon'))  80 us
    unnamed x13, other arithmetic  66.9 us
    sub x4, other arithmetic, forward_step(): return field + vertical(field, mixing) - div_lon - div_lat  43 us
    add x3, other arithmetic, reverse_step(): return adjoint + vertical(adjoint, mixing) + back_lon + back_lat  22.9 us
    unnamed x143, local copies, waits for them, and re-layouts  17.7 us
    slice x6, local copies, waits for them, and re-layouts, reverse_step(): east = jnp.roll(adjoint, -1, 2)  17.2 us
    slice x8, local copies, waits for them, and re-layouts, forward_step(): west = jnp.roll(field, 1, 2)  17.1 us
  transfers between devices with their start and end apart: 4, of which 3 were waited for; matrix products, arithmetic and copies ran while one was open for 2% of the time, Pallas kernels for 0%

profile of v1, /device:TPU:6, one launch (start us, length us, event | category | flops | bytes accessed | tf_op | source)
XLA Modules:
  0.0 668.2 jit_solution(1586393645362922137)
XLA Ops:
  18.6 4.1 collective-permute-done.1
  30.2 4.6 pad_maximum_fusion.1
  51.2 7.5 %collective-permute-start.3 = (f32[380928]{0:T(1024)}, f32[380928]{0:T(1024)}, u32[]{:S(2)}, u32[]{:S(2)}) collective-permute-start(f32[380928]{0:T(1024)} %get-tuple-element.166), channel_id=1, source_target_pairs={{16,0},{32,16},{48,32},{64,48},{80,64},{96,80},{112,96},{128,112},... | collective-permute-start | bytes 4571144 | tf_op jit(solution)/shard_map/ppermute | solution.py:32
  59.9 14.5 %collective-permute-done.2 = f32[380928]{0:T(1024)} collective-permute-done((f32[380928]{0:T(1024)}, f32[380928]{0:T(1024)}, u32[]{:S(2)}, u32[]{:S(2)}) %collective-permute-start.2) | collective-permute-done | bytes 1523744 | tf_op jit(solution)/shard_map/ppermute | solution.py:31
  77.0 4.0 reshape.1017
  87.5 6.3 pad_maximum_fusion
  93.8 4.4 slice_bitcast_fusion.2
  120.5 10.2 %fusion.4 = f32[64,32,144]{2,1,0:T(8,128)S(1)} fusion(f32[64,32,1]{2,1,0:T(8,128)} %get-tuple-element.112, f32[64,32,143]{2,1,0:T(8,128)} %get-tuple-element.114, f32[64,32,143]{2,1,0:T(8,128)} %get-tuple-element.113, f32[64,32,1]{2,1,0:T(8,128)} %get-tuple-element.111, f32[64,1,144]{2,1,0:T(1,128)S(1)} %get-tuple-element.108, ...), kind=kLoop, calls=%fused_computation.31 | loop fusion | flops 7372800 | bytes 17676288 | tf_op jit(solution)/shard_map/sub | solution.py:102
  138.9 9.6 %fusion.12 = f32[64,32,144]{2,1,0:T(8,128)S(1)} fusion(f32[64,32,1]{2,1,0:T(8,128)} %get-tuple-element.104, f32[64,32,143]{2,1,0:T(8,128)} %get-tuple-element.106, f32[64,32,143]{2,1,0:T(8,128)} %get-tuple-element.105, f32[64,32,1]{2,1,0:T(8,128)S(1)} %get-tuple-element.103, f32[64,1,144]{2,1,0:T(1,128)S(1)} %get-tuple-element.100, ...), kind=kLoop, calls=%fused_computation.44 | loop fusion | flops 7372800 | bytes 17676288 | tf_op jit(solution)/shard_map/sub | solution.py:102
  159.7 9.8 %fusion.20 = f32[64,32,144]{2,1,0:T(8,128)S(1)} fusion(f32[64,32,1]{2,1,0:T(8,128)} %get-tuple-element.96, f32[64,32,143]{2,1,0:T(8,128)} %get-tuple-element.98, f32[64,32,143]{2,1,0:T(8,128)} %get-tuple-element.97, f32[64,32,1]{2,1,0:T(8,128)S(1)} %get-tuple-element.95, f32[64,1,144]{2,1,0:T(1,128)S(1)} %get-tuple-element.92, ...), kind=kLoop, calls=%fused_computation.56 | loop fusion | flops 7372800 | bytes 17676288 | tf_op jit(solution)/shard_map/sub | solution.py:102
  192.0 22.2 %gather_fusion.3 = f32[2304]{0:T(1024)S(1)} fusion(f32[64,32,144]{2,1,0:T(8,128)S(1)} %fusion.4, s32[2304]{0:T(1024)S(1)} %reshape.1065), kind=kCustom, calls=%fused_computation.3 | custom fusion | bytes 46080 | tf_op jit(solution)/shard_map/gather | solution.py:123
  214.3 77.3 %gather_fusion.2 = f32[2304]{0:T(1024)S(1)} fusion(f32[64,32,144]{2,1,0:T(8,128)} %copy-done, s32[2304]{0:T(1024)S(1)} %reshape.1059), kind=kCustom, calls=%fused_computation.2 | custom fusion | bytes 46080 | tf_op jit(solution)/shard_map/gather | solution.py:123
  292.2 22.4 %gather_fusion.1 = f32[2304]{0:T(1024)S(1)} fusion(f32[64,32,144]{2,1,0:T(8,128)S(1)} %copy-done.2, s32[2304]{0:T(1024)S(1)} %reshape.1053), kind=kCustom, calls=%fused_computation.1 | custom fusion | bytes 46080 | tf_op jit(solution)/shard_map/gather | solution.py:123
  314.6 13.4 %fusion.28 = f32[64,32,144]{2,1,0:T(8,128)} fusion(f32[64,32,1]{2,1,0:T(8,128)} %get-tuple-element.88, f32[64,32,143]{2,1,0:T(8,128)} %get-tuple-element.90, f32[64,32,143]{2,1,0:T(8,128)} %get-tuple-element.89, f32[64,32,1]{2,1,0:T(8,128)} %get-tuple-element.87, f32[64,1,144]{2,1,0:T(1,128)} %get-tuple-element.84, f32[64,31,144]{2,1,0:T(8,128)} %get-tuple-element.86, ...), kind=kLoop, calls=%fused_computation.68 | loop fusion | flops 7372800 | bytes 17676288 | tf_op jit(solution)/shard_map/sub | solution.py:102
  328.2 81.1 %gather_fusion = f32[2304]{0:T(1024)S(1)} fusion(f32[64,32,144]{2,1,0:T(8,128)} %fusion.28, s32[2304]{0:T(1024)S(1)} %reshape.1047), kind=kCustom, calls=%fused_computation | custom fusion | bytes 46080 | tf_op jit(solution)/shard_map/gather | solution.py:123
  410.8 15.5 %scatter_custom_fusion = f32[294912]{0:T(1024)S(1)} fusion(s32[2304]{0:T(1024)} %reshape.1071, f32[2304]{0:T(1024)S(1)} %reshape.1073, f32[]{:T(128)} %constant.30.clone.1), kind=kCustom, calls=%fused_computation.126 | custom fusion | flops 2304 | bytes 1180160
  441.3 9.3 %subtract_negate_fusion = (f32[64,32,144]{2,1,0:T(8,128)}, f32[64,32,144]{2,1,0:T(8,128)}) fusion(f32[64,1,144]{2,1,0:T(1,128)S(1)} %slice.1239, f32[64,31,144]{2,1,0:T(8,128)S(1)} %copy-done.6, f32[5,64,32,144]{3,2,1,0:T(8,128)} %copy-done.3, f32[64,1,144]{2,1,0:T(1,128)S(1)} %get-tuple-element.77, f32[64,31,144]{2,1,0:T(8,128)} %get-tuple-element.75, ...), kind=kLoop, calls=%fused_computation.105 | loop fusion | flops 6782976 | bytes 14137344 | tf_op jit(solution)/shard_map/neg | solution.py:110
  453.4 15.6 %scatter_fusion = f32[294912]{0:T(1024)S(1)} fusion(f32[294912]{0:T(1024)S(1)} %reshape.1024, s32[2304]{0:T(1024)S(1)} %reshape.1077, f32[2304]{0:T(1024)S(1)} %reshape.1079), kind=kCustom, calls=%fused_computation.5 | custom fusion | flops 2304 | bytes 36864
  487.9 8.0 %fusion.41 = f32[64,32,144]{2,1,0:T(8,128)} fusion(f32[64,32,143]{2,1,0:T(8,128)} %get-tuple-element.72, f32[64,32,1]{2,1,0:T(8,128)} %get-tuple-element.74, f32[64,32,144]{2,1,0:T(8,128)S(1)} %copy-done.8, f32[64,32,1]{2,1,0:T(8,128)S(1)} %copy-done.28, f32[64,32,143]{2,1,0:T(8,128)} %get-tuple-element.71, f32[64,31,144]{2,1,0:T(8,128)} %get-tuple-element.68, ...), kind=kLoop, calls=%fused_computation.89 | loop fusion | flops 6782976 | bytes 12957696 | tf_op jit(solution)/shard_map/add | solution.py:111
  498.7 15.6 %scatter_fusion.1 = f32[294912]{0:T(1024)S(1)} fusion(f32[294912]{0:T(1024)S(1)} %reshape.1028, s32[2304]{0:T(1024)S(1)} %reshape.1083, f32[2304]{0:T(1024)S(1)} %reshape.1085), kind=kCustom, calls=%fused_computation.6 | custom fusion | flops 2304 | bytes 36864
  533.3 8.0 %fusion.47 = f32[64,32,144]{2,1,0:T(8,128)} fusion(f32[64,32,143]{2,1,0:T(8,128)} %get-tuple-element.64, f32[64,32,1]{2,1,0:T(8,128)} %get-tuple-element.66, f32[64,32,144]{2,1,0:T(8,128)S(1)} %copy-done.9, f32[64,32,1]{2,1,0:T(8,128)S(1)} %copy-done.27, f32[64,32,143]{2,1,0:T(8,128)} %get-tuple-element.63, f32[64,31,144]{2,1,0:T(8,128)} %get-tuple-element.60, ...), kind=kLoop, calls=%fused_computation.99 | loop fusion | flops 6782976 | bytes 12957696 | tf_op jit(solution)/shard_map/add | solution.py:111
  544.1 15.4 %scatter_fusion.2 = f32[294912]{0:T(1024)S(1)} fusion(f32[294912]{0:T(1024)S(1)} %reshape.1032, s32[2304]{0:T(1024)S(1)} %reshape.1089, f32[2304]{0:T(1024)S(1)} %reshape.1091), kind=kCustom, calls=%fused_computation.7 | custom fusion | flops 2304 | bytes 36864
  575.7 80.0 %psum.7 = f32[]{:T(128)} all-reduce(f32[]{:T(128)S(6)} %add.382), channel_id=1, replica_groups=mesh['lat'=16,'lon'=16] {'lat','lon'}, use_global_device_ids=true, to_apply=%region_8.9 | all-reduce | flops 1 | bytes 8 | tf_op jit(solution)/shard_map/psum | solution.py:135
  660.8 7.0 %fusion.60 = f32[64,16,128]{2,1,0:T(8,128)} fusion(f32[64,31,144]{2,1,0:T(8,128)S(1)} %copy-done.6, f32[64,32,143]{2,1,0:T(8,128)S(1)} %copy-done.17, f32[64,32,1]{2,1,0:T(8,128)S(1)} %copy-done.22, f32[64,1,144]{2,1,0:T(1,128)S(1)} %slice.1239, f32[64,1,144]{2,1,0:T(1,128)S(1)} %get-tuple-element.56, f32[64,31,144]{2,1,0:T(8,128)} %get-tuple-element.58, ...), kind=kLoop, calls=%fused_computation.131 | loop fusion | flops 2621440 | bytes 11384832 | tf_op jit(solution)/shard_map/add | solution.py:111
  (278 shorter events, 197.9 us)
Async XLA Ops:
  15.5 7.3 %collective-permute-start.1 = (f32[45056]{0:T(1024)S(1)}, f32[45056]{0:T(1024)S(1)}, u32[]{:S(2)}, u32[]{:S(2)}) collective-permute-start(f32[45056]{0:T(1024)S(1)} %get-tuple-element.172), channel_id=1, source_target_pairs={{1,0},{2,1},{3,2},{4,3},{5,4},{6,5},{7,6},{8,7},{9,8},{10,9},{11,1... | collective-permute-start | bytes 540680 | tf_op jit(solution)/shard_map/ppermute | solution.py:32
  16.4 10.9 %collective-permute-start = (f32[45056]{0:T(1024)S(1)}, f32[45056]{0:T(1024)S(1)}, u32[]{:S(2)}, u32[]{:S(2)}) collective-permute-start(f32[45056]{0:T(1024)S(1)} %get-tuple-element.171), channel_id=1, source_target_pairs={{0,1},{1,2},{2,3},{3,4},{4,5},{5,6},{6,7},{7,8},{8,9},{9,10},{10,1... | collective-permute-start | bytes 540680 | tf_op jit(solution)/shard_map/ppermute | solution.py:31
  49.3 25.1 %collective-permute-start.2 = (f32[380928]{0:T(1024)}, f32[380928]{0:T(1024)}, u32[]{:S(2)}, u32[]{:S(2)}) collective-permute-start(f32[380928]{0:T(1024)} %get-tuple-element.165), channel_id=1, source_target_pairs={{0,16},{16,32},{32,48},{48,64},{64,80},{80,96},{96,112},{112,128},... | collective-permute-start | bytes 4571144 | tf_op jit(solution)/shard_map/ppermute | solution.py:31
  51.2 29.8 %collective-permute-start.3 = (f32[380928]{0:T(1024)}, f32[380928]{0:T(1024)}, u32[]{:S(2)}, u32[]{:S(2)}) collective-permute-start(f32[380928]{0:T(1024)} %get-tuple-element.166), channel_id=1, source_target_pairs={{16,0},{32,16},{48,32},{64,48},{80,64},{96,80},{112,96},{128,112},... | collective-permute-start | bytes 4571144 | tf_op jit(solution)/shard_map/ppermute | solution.py:32
  93.8 45.1 %copy-start.3 = (f32[5,64,32,144]{3,2,1,0:T(8,128)}, f32[5,64,32,144]{3,2,1,0:T(8,128)S(1)}, u32[]{:S(2)}) copy-start(f32[5,64,32,144]{3,2,1,0:T(8,128)S(1)} %pad_maximum_fusion) | copy-start | bytes 17694724
  102.0 18.6 %copy-start.4 = (f32[64,31,144]{2,1,0:T(8,128)}, f32[64,31,144]{2,1,0:T(8,128)S(1)}, u32[]{:S(2)}) copy-start(f32[64,31,144]{2,1,0:T(8,128)S(1)} %slice.1238) | copy-start | bytes 3428356
  102.3 15.4 %copy-start.21 = (f32[64,32,1]{2,1,0:T(8,128)}, f32[64,32,1]{2,1,0:T(8,128)S(1)}, u32[]{:S(2)}) copy-start(f32[64,32,1]{2,1,0:T(8,128)S(1)} %slice.1229) | copy-start | bytes 24580
  214.2 78.0 %copy-start.2 = (f32[64,32,144]{2,1,0:T(8,128)S(1)}, f32[64,32,144]{2,1,0:T(8,128)}, u32[]{:S(2)}) copy-start(f32[64,32,144]{2,1,0:T(8,128)} %copy-done.1) | copy-start | bytes 3538948
  328.0 81.3 %copy-start.43 = (f32[1,4,256]{2,0,1:T(1,128)S(1)}, f32[1,4,256]{2,0,1:T(1,128)}, u32[]{:S(2)}) copy-start(f32[1,4,256]{2,0,1:T(1,128)} %copy-done.42) | copy-start | bytes 12292
  328.0 81.3 %copy-start.46 = (f32[1024]{0:T(1024)S(1)}, f32[1024]{0:T(1024)}, u32[]{:S(2)}) copy-start(f32[1024]{0:T(1024)} %get-tuple-element.128) | copy-start | bytes 12292
  328.1 81.3 %copy-start.47 = (f32[1024]{0:T(1024)S(1)}, f32[1024]{0:T(1024)}, u32[]{:S(2)}) copy-start(f32[1024]{0:T(1024)} %get-tuple-element.129) | copy-start | bytes 12292
  328.1 81.3 %copy-start.48 = (f32[1024]{0:T(1024)S(1)}, f32[1024]{0:T(1024)}, u32[]{:S(2)}) copy-start(f32[1024]{0:T(1024)} %get-tuple-element.130) | copy-start | bytes 12292
  328.1 81.3 %copy-start.49 = (f32[1024]{0:T(1024)S(1)}, f32[1024]{0:T(1024)}, u32[]{:S(2)}) copy-start(f32[1024]{0:T(1024)} %get-tuple-element.116) | copy-start | bytes 12292
  328.1 81.3 %copy-start.50 = (f32[1024]{0:T(1024)S(1)}, f32[1024]{0:T(1024)}, u32[]{:S(2)}) copy-start(f32[1024]{0:T(1024)} %get-tuple-element.117) | copy-start | bytes 12292
  328.1 81.3 %copy-start.51 = (f32[1024]{0:T(1024)S(1)}, f32[1024]{0:T(1024)}, u32[]{:S(2)}) copy-start(f32[1024]{0:T(1024)} %get-tuple-element.118) | copy-start | bytes 12292
  328.1 81.3 %copy-start.53 = (f32[1024]{0:T(1024)S(1)}, f32[1024]{0:T(1024)}, u32[]{:S(2)}) copy-start(f32[1024]{0:T(1024)} %get-tuple-element.156) | copy-start | bytes 12292
  328.1 81.3 %copy-start.54 = (f32[1024]{0:T(1024)S(1)}, f32[1024]{0:T(1024)}, u32[]{:S(2)}) copy-start(f32[1024]{0:T(1024)} %get-tuple-element.152) | copy-start | bytes 12292
  328.1 81.3 %copy-start.33 = (f32[9,256]{1,0:T(8,128)S(1)}, f32[9,256]{1,0:T(8,128)}, u32[]{:S(2)}) copy-start(f32[9,256]{1,0:T(8,128)} %reshape.1062) | copy-start | bytes 27652
  328.1 81.3 %copy-start.38 = (f32[9,1,256]{2,1,0:T(1,128)S(1)}, f32[9,1,256]{2,1,0:T(1,128)}, u32[]{:S(2)}) copy-start(f32[9,1,256]{2,1,0:T(1,128)} %get-tuple-element.167) | copy-start | bytes 27652
  328.2 81.3 %copy-start.39 = (f32[9,1,256]{2,1,0:T(1,128)S(1)}, f32[9,1,256]{2,1,0:T(1,128)}, u32[]{:S(2)}) copy-start(f32[9,1,256]{2,1,0:T(1,128)} %get-tuple-element.168) | copy-start | bytes 27652
  328.2 81.3 %copy-start.40 = (f32[9,1,256]{2,1,0:T(1,128)S(1)}, f32[9,1,256]{2,1,0:T(1,128)}, u32[]{:S(2)}) copy-start(f32[9,1,256]{2,1,0:T(1,128)} %get-tuple-element.169) | copy-start | bytes 27652
  328.2 81.3 %copy-start.41 = (f32[9,1,256]{2,1,0:T(1,128)S(1)}, f32[9,1,256]{2,1,0:T(1,128)}, u32[]{:S(2)}) copy-start(f32[9,1,256]{2,1,0:T(1,128)} %get-tuple-element.170) | copy-start | bytes 27652
  328.2 81.3 %copy-start.62 = (pred[9]{0:T(512)(128)(4,1)S(1)}, pred[9]{0:T(512)(128)(4,1)}, u32[]{:S(2)}) copy-start(pred[9]{0:T(512)(128)(4,1)} %constant.90.clone) | copy-start | bytes 31
  569.1 86.6 %copy-start.23 = (f32[290304]{0:T(1024)S(1)}, f32[290304]{0:T(1024)}, u32[]{:S(2)}) copy-start(f32[290304]{0:T(1024)} %slice_subtract_fusion.4) | copy-start | bytes 3483652
  (43 other events, 164.9 us)
